TPU v7x, 32 devices: a whole 2x2x4 slice. The times are simulated.
32 devices in a mesh: dp: 2 (over x), mp: 16 (over z, y, core).
Axes of the slice: x: 2, y: 2, z: 4, core: 2. Of those that a mesh axis runs over, the one named last changes fastest.
Arguments:
- node_features: bfloat16 [512, 6144], P('mp', 'dp'), may hold values from -6 to 6
- weights_one: bfloat16 [1024, 512], replicated, may hold values from -0.25 to 0.25
- weights_two: bfloat16 [1024, 512], replicated, may hold values from -0.25 to 0.25
- neighbor_owner: int32 [6144, 8], P('dp'), may hold values from 0 to 15, all different within a row; in each aligned block of 192 rows (0 to 191, 192 to 383, ...) at most 144 rows name the same one
- neighbor_row: int32 [6144, 8], P('dp'), may hold values from 0 to 191
- neighbor_count: int32 [6144], P('dp'), may hold values from 4 to 8
- cotangent: bfloat16 [6144, 512], P(('dp', 'mp')), may hold values from -0.076171875 to 0.076171875
Outputs:
- node_output: bfloat16 [6144, 512], P(('dp', 'mp'))
- weight_grads: float32 [2048, 512], P(('dp', 'mp'))
Inputs may be any that keep to these rules, and one draw needn't show every extreme that they name: `neighbor_owner`: each row names 8 different owners; among the rows of one device (aligned blocks of 192 rows) no owner is named more than 144 times, and in some block one owner exactly 144 times. Slots k >= neighbor_count[r] are padding and carry no edge.
All inputs are finite; a program needn't handle non-finite values.
Results may differ from a plain program's by a relative error of at most 0.0052.
Values may be sent and summed in bfloat16 or wider, within the bound.
No kernel may reach another device: no remote copies, remote signals or barrier semaphores. Data moves between devices by JAX's collectives and lax.ppermute only.
A program may use at most 64 MiB of HBM per device.

v0:
```python
import jax
import jax.numpy as jnp
from jax import lax
from jax.sharding import PartitionSpec as P


def column_mean(table, indices, live, inverse):
    total = jnp.zeros((table.shape[0], indices.shape[1]), jnp.float32)
    for slot_index in range(indices.shape[0]):
        picked = jnp.take(table, indices[slot_index], axis=1)
        kept = jnp.where(live[slot_index][None, :], picked, jnp.zeros_like(picked))
        total = total + kept.astype(jnp.float32)
    return (total * inverse[None, :]).astype(jnp.bfloat16)


def silu_slope(values):
    sigmoid = jax.nn.sigmoid(values)
    return sigmoid * (1.0 + values * (1.0 - sigmoid))


def contract(left, right, left_dim, right_dim):
    return lax.dot_general(
        left, right, (((left_dim,), (right_dim,)), ((), ())), preferred_element_type=jnp.float32
    )


def shards(
    node_features, weights_one, weights_two, neighbor_owner, neighbor_row, neighbor_count, cotangent
):
    devices = lax.axis_size("mp")
    own_index = lax.axis_index("mp")
    node_dev = cotangent.shape[0]
    all_nodes = neighbor_owner.shape[0]
    fanout = neighbor_owner.shape[1]
    feat_width = weights_one.shape[0] // 2
    hidden = weights_one.shape[1]
    capacity = 3 * node_dev * fanout // (2 * devices)
    live = lax.broadcasted_iota(jnp.int32, (all_nodes, fanout), 1) < neighbor_count[:, None]
    inverse_all = 1.0 / neighbor_count.astype(jnp.float32)
    owner_ids = lax.broadcasted_iota(jnp.int32, (devices, 1, 1), 0)
    match = (neighbor_owner[None, :, :] == owner_ids) & live[None, :, :]
    rowsel = jnp.max(jnp.where(match, neighbor_row[None, :, :], -1), axis=2)
    has = rowsel >= 0
    with jax.named_scope("layer_one_mean"):
        if all_nodes * all_nodes <= 4096 * 4096:
            row_ids = lax.broadcasted_iota(jnp.int32, (1, node_dev, 1), 1)
            adjacency = (rowsel[:, None, :] == row_ids).astype(jnp.bfloat16)
            adjacency = adjacency.reshape(devices * node_dev, all_nodes)
            summed = contract(node_features, adjacency, 1, 0)
            agg_one_cols = (summed * inverse_all[None, :]).astype(jnp.bfloat16)
        else:
            owner_slots = neighbor_owner.T
            global_ids = owner_slots * node_dev + neighbor_row.T
            agg_one_cols = column_mean(node_features, global_ids, live.T, inverse_all)
    own_feats, own_agg_one = (
        lax.all_to_all(node_features, "mp", split_axis=1, concat_axis=0, tiled=True),
        lax.all_to_all(agg_one_cols, "mp", split_axis=1, concat_axis=0, tiled=True),
    )
    pre_one = contract(weights_one[:feat_width], own_feats, 0, 0) + contract(
        weights_one[feat_width:], own_agg_one, 0, 0
    )
    hidden_one = jax.nn.silu(pre_one).astype(jnp.bfloat16)
    with jax.named_scope("slot_tables"):
        blocks = has.reshape(devices * devices, node_dev).astype(jnp.bfloat16)
        before = (
            lax.broadcasted_iota(jnp.int32, (node_dev, node_dev), 0)
            < lax.broadcasted_iota(jnp.int32, (node_dev, node_dev), 1)
        ).astype(jnp.bfloat16)
        ranks = contract(blocks, before, 1, 0).astype(jnp.int32).reshape(devices, devices, node_dev)
        has_blocks = has.reshape(devices, devices, node_dev)
        rows_blocks = rowsel.reshape(devices, devices, node_dev)
        cap_ids = lax.broadcasted_iota(jnp.int32, (1, capacity, 1), 1)
        own_rank = lax.dynamic_index_in_dim(ranks, own_index, 1, keepdims=False)
        own_has = lax.dynamic_index_in_dim(has_blocks, own_index, 1, keepdims=False)
        gathered = ((own_rank[:, None, :] == cap_ids) & own_has[:, None, :]).astype(jnp.bfloat16)
        gathered = gathered.reshape(devices * capacity, node_dev)
        req_rank = lax.dynamic_index_in_dim(ranks, own_index, 0, keepdims=False)
        req_has = lax.dynamic_index_in_dim(has_blocks, own_index, 0, keepdims=False)
        req_rows = lax.dynamic_index_in_dim(rows_blocks, own_index, 0, keepdims=False)
        pick = ((req_rank[:, None, :] == cap_ids) & req_has[:, None, :]).astype(jnp.bfloat16)
        row_ids = lax.broadcasted_iota(jnp.int32, (1, 1, node_dev), 2)
        which = (req_rows[:, :, None] == row_ids).astype(jnp.bfloat16)
        asked = lax.dot_general(
            pick, which, (((2,), (1,)), ((0,), (0,))), preferred_element_type=jnp.float32
        )
        asked = asked.astype(jnp.bfloat16).reshape(devices * capacity, node_dev)
    own_inverse = lax.dynamic_slice_in_dim(inverse_all, own_index * node_dev, node_dev, 0)
    outgoing = contract(hidden_one, asked, 1, 1).astype(jnp.bfloat16)
    incoming = lax.all_to_all(outgoing, "mp", split_axis=1, concat_axis=1, tiled=True)
    total = contract(incoming, gathered, 1, 0)
    agg_two = (total * own_inverse[None, :]).astype(jnp.bfloat16)
    self_two = weights_two[:hidden]
    neigh_two = weights_two[hidden:]
    node_output = (
        contract(hidden_one, self_two, 0, 0) + contract(agg_two, neigh_two, 0, 0)
    ).astype(jnp.bfloat16)
    down_self = contract(self_two, cotangent, 1, 1)
    down_neigh = (contract(neigh_two, cotangent, 1, 1) * own_inverse[None, :]).astype(jnp.bfloat16)
    outgoing_grad = contract(down_neigh, gathered, 1, 1).astype(jnp.bfloat16)
    incoming_grad = lax.all_to_all(outgoing_grad, "mp", split_axis=1, concat_axis=1, tiled=True)
    neighbor_sum = contract(incoming_grad, asked, 1, 0)
    grad_hidden = down_self + neighbor_sum
    grad_pre = (grad_hidden * silu_slope(pre_one)).astype(jnp.bfloat16)
    terms = jnp.concatenate(
        [
            contract(own_feats, grad_pre, 1, 1),
            contract(own_agg_one, grad_pre, 1, 1),
            contract(hidden_one, cotangent, 1, 0),
            contract(agg_two, cotangent, 1, 0),
        ],
        axis=0,
    )
    weight_grads = lax.psum_scatter(terms, ("dp", "mp"), scatter_dimension=0, tiled=True)
    return (node_output, weight_grads)


def solution(mesh):
    in_specs = (
        P("mp", "dp"),
        P(),
        P(),
        P("dp", None),
        P("dp", None),
        P("dp"),
        P(("dp", "mp"), None),
    )
    out_specs = (P(("dp", "mp"), None), P(("dp", "mp"), None))
    return jax.shard_map(shards, mesh=mesh, in_specs=in_specs, out_specs=out_specs, check_vma=False)
```

profile of v0, /device:TPU:0, one launch (start us, length us, event | category | flops | bytes accessed | tf_op | source)
XLA Modules:
  0.0 325.1 jit_solution(16609977738096543799)
XLA Ops:
  7.2 1.3 all_to_all.40
  8.5 0.8 copy.27
  9.3 7.4 %all-to-all-start = ((bf16[32,16,192]{2,0,1:T(8,128)(2,1)}), bf16[32,16,192]{2,0,1:T(8,128)(2,1)S(1)}, u32[]{:S(2)}, u32[]{:S(2)}) async-start(bf16[32,16,192]{2,0,1:T(8,128)(2,1)} %copy.27), calls=%async_computation | async-start | bytes 524288 | tf_op jit(solution)/shard_map/all_to_all | solution.py:56
  16.7 0.7 iota_compare_fusion.9
  17.4 0.7 convert_divide_fusion
  18.2 1.8 select_reduce_fusion
  20.0 9.7 %bitcast_compare_fusion = pred[3072,3072]{1,0:T(32,128)(4,1)} fusion(s32[3072]{0:T(1024)S(1)} %eq.95, s32[16,3072]{1,0:T(8,128)S(1)} %select_reduce_fusion), kind=kLoop, calls=%fused_computation | loop fusion | flops 9437184 | bytes 9646080 | tf_op jit(solution)/shard_map/layer_one_mean/eq | solution.py:47
  29.9 8.5 %fusion.1 = bf16[32,3072]{1,0:T(8,128)(2,1)S(1)} fusion(pred[3072,3072]{1,0:T(32,128)(4,1)} %bitcast_compare_fusion, bf16[32,3072]{1,0:T(8,128)(2,1)S(1)} %copy-done.7, f32[3072]{0:T(1024)S(1)} %convert_divide_fusion), kind=kOutput, calls=%fused_computation.6 | convolution fusion | flops 604176384 | bytes 9842688 | tf_op jit(solution)/shard_map/layer_one_mean/dot_general | solution.py:22
  38.4 0.4 convolution_convert_fusion.2
  39.3 0.8 copy.28
  40.4 6.1 %all-to-all-start.1 = ((bf16[32,16,192]{2,0,1:T(8,128)(2,1)}), bf16[32,16,192]{2,0,1:T(8,128)(2,1)}, u32[]{:S(2)}, u32[]{:S(2)}) async-start(bf16[32,16,192]{2,0,1:T(8,128)(2,1)} %copy.28), calls=%async_computation.1 | async-start | bytes 524288 | tf_op jit(solution)/shard_map/all_to_all | solution.py:57
  46.7 0.5 fusion.8
  47.2 2.2 convolution_convert_fusion
  49.4 2.5 copy.31
  51.9 4.6 %all-to-all-done.1 = bf16[32,16,192]{2,0,1:T(8,128)(2,1)} async-done(((bf16[32,16,192]{2,0,1:T(8,128)(2,1)}), bf16[32,16,192]{2,0,1:T(8,128)(2,1)}, u32[]{:S(2)}, u32[]{:S(2)}) %all-to-all-start.1) | async-done | bytes 196640 | tf_op jit(solution)/shard_map/all_to_all | solution.py:57
  56.5 3.7 %all-to-all-start.3 = ((bf16[512,16,144]{0,2,1:T(8,128)(2,1)}), bf16[512,16,144]{0,2,1:T(8,128)(2,1)S(1)}, u32[]{:S(2)}, u32[]{:S(2)}) async-start(bf16[512,16,144]{0,2,1:T(8,128)(2,1)} %bitcast.16), calls=%async_computation.3 | async-start | bytes 4718592 | tf_op jit(solution)/shard_map/all_to_all | solution.py:100
  60.3 0.8 dynamic-slice_bitcast_fusion
  61.1 1.3 fusion.11
  62.8 1.3 fusion.18
  64.1 2.4 convolution_convert_fusion.1
  66.5 4.3 %copy.30 = bf16[512,2304]{0,1:T(8,128)(2,1)} copy(bf16[512,2304]{1,0:T(8,128)(2,1)} %convolution_convert_fusion.1) | data formatting | bytes 4718592 | tf_op jit(solution)/shard_map/convert_element_type | solution.py:88
  70.8 35.1 %all-to-all-done.3 = bf16[512,16,144]{0,2,1:T(8,128)(2,1)S(1)} async-done(((bf16[512,16,144]{0,2,1:T(8,128)(2,1)}), bf16[512,16,144]{0,2,1:T(8,128)(2,1)S(1)}, u32[]{:S(2)}, u32[]{:S(2)}) %all-to-all-start.3) | async-done | bytes 2359328 | tf_op jit(solution)/shard_map/all_to_all | solution.py:100
  105.9 12.3 %all-to-all-start.2 = ((bf16[512,16,144]{0,2,1:T(8,128)(2,1)}), bf16[512,16,144]{0,2,1:T(8,128)(2,1)}, u32[]{:S(2)}, u32[]{:S(2)}) async-start(bf16[512,16,144]{0,2,1:T(8,128)(2,1)} %bitcast.12), calls=%async_computation.2 | async-start | bytes 4718592 | tf_op jit(solution)/shard_map/all_to_all | solution.py:89
  118.2 1.4 fusion.42
  119.6 2.0 convolution_bitcast_fusion.1
  122.0 1.2 fusion.43
  123.5 40.4 %all-to-all-done.2 = bf16[512,16,144]{0,2,1:T(8,128)(2,1)} async-done(((bf16[512,16,144]{0,2,1:T(8,128)(2,1)}), bf16[512,16,144]{0,2,1:T(8,128)(2,1)}, u32[]{:S(2)}, u32[]{:S(2)}) %all-to-all-start.2) | async-done | bytes 2359328 | tf_op jit(solution)/shard_map/all_to_all | solution.py:89
  163.9 2.6 fusion.26
  166.9 2.4 pad_maximum_fusion
  169.3 1.2 copy-done.4
  170.8 1.0 fusion.30
  171.7 146.5 %reduce-scatter.2.cloned.1.call-done = f32[64,512]{1,0:T(8,128)} async-done(((f32[2048,512]{1,0:T(8,128)}), f32[64,512]{1,0:T(8,128)}) %reduce-scatter.2.cloned.1.call-update) | async-done | bytes 131088 | tf_op jit(solution)/shard_map/reduce_scatter | solution.py:113
  (41 shorter events, 2.8 us)
Async XLA Ops:
  7.2 40.0 %copy-start = (bf16[192,512]{1,0:T(8,128)(2,1)S(1)}, bf16[192,512]{1,0:T(8,128)(2,1)}, u32[]{:S(2)}) copy-start(bf16[192,512]{1,0:T(8,128)(2,1)} %param.13) | copy-start | bytes 589828
  9.3 31.1 %all-to-all-start = ((bf16[32,16,192]{2,0,1:T(8,128)(2,1)}), bf16[32,16,192]{2,0,1:T(8,128)(2,1)S(1)}, u32[]{:S(2)}, u32[]{:S(2)}) async-start(bf16[32,16,192]{2,0,1:T(8,128)(2,1)} %copy.27), calls=%async_computation | async-start | bytes 524288 | tf_op jit(solution)/shard_map/all_to_all | solution.py:56
  20.0 9.9 %copy-start.7 = (bf16[32,3072]{1,0:T(8,128)(2,1)S(1)}, bf16[32,3072]{1,0:T(8,128)(2,1)}, u32[]{:S(2)}) copy-start(bf16[32,3072]{1,0:T(8,128)(2,1)} %param.7) | copy-start | bytes 589828
  39.0 7.7 %copy-start.1 = (s32[16,16,192]{2,1,0:T(8,128)}, s32[16,16,192]{2,1,0:T(8,128)S(1)}, u32[]{:S(2)}) copy-start(s32[16,16,192]{2,1,0:T(8,128)S(1)} %reduce_max.12) | copy-start | bytes 589828
  40.2 6.4 %copy-start.6 = (s32[256,192]{1,0:T(8,128)}, s32[256,192]{1,0:T(8,128)S(1)}, u32[]{:S(2)}) copy-start(s32[256,192]{1,0:T(8,128)S(1)} %copy.29) | copy-start | bytes 589828
  40.4 16.2 %all-to-all-start.1 = ((bf16[32,16,192]{2,0,1:T(8,128)(2,1)}), bf16[32,16,192]{2,0,1:T(8,128)(2,1)}, u32[]{:S(2)}, u32[]{:S(2)}) async-start(bf16[32,16,192]{2,0,1:T(8,128)(2,1)} %copy.28), calls=%async_computation.1 | async-start | bytes 524288 | tf_op jit(solution)/shard_map/all_to_all | solution.py:57
  56.5 49.3 %all-to-all-start.3 = ((bf16[512,16,144]{0,2,1:T(8,128)(2,1)}), bf16[512,16,144]{0,2,1:T(8,128)(2,1)S(1)}, u32[]{:S(2)}, u32[]{:S(2)}) async-start(bf16[512,16,144]{0,2,1:T(8,128)(2,1)} %bitcast.16), calls=%async_computation.3 | async-start | bytes 4718592 | tf_op jit(solution)/shard_map/all_to_all | solution.py:100
  60.3 2.2 copy-start.2
  62.5 1.7 copy-start.8
  105.9 58.0 %all-to-all-start.2 = ((bf16[512,16,144]{0,2,1:T(8,128)(2,1)}), bf16[512,16,144]{0,2,1:T(8,128)(2,1)}, u32[]{:S(2)}, u32[]{:S(2)}) async-start(bf16[512,16,144]{0,2,1:T(8,128)(2,1)} %bitcast.12), calls=%async_computation.2 | async-start | bytes 4718592 | tf_op jit(solution)/shard_map/all_to_all | solution.py:89
  118.2 200.1 %reduce-scatter.2.cloned.1.call-start = ((), (), s32[]{:S(2)}) async-start(), calls=%async_computation.5 | async-start | bytes 4325376 | tf_op jit(solution)/shard_map/reduce_scatter | solution.py:113
  119.6 2.0 copy-start.3
  163.9 3.0 copy-start.5
  169.3 1.2 copy-start.4
Sparse Core Ops, SparseCore 0:
  169.4 148.7 reduce-scatter.1
where the time goes:
time: 326 us; the launch traced here: 325 us
  waiting for transfers between devices  227 us (70%)
  starting transfers between devices  29.5 us (9%)
  matrix products  25.9 us (8%)
  other arithmetic  15.9 us (5%)
  between operations  14.4 us (4%)
  local copies, waits for them, and re-layouts  12.7 us (4%)
    reduce_scatter x1, waiting for transfers between devices, shards(): lax.psum_scatter(terms, ('dp', 'mp'), scatter_dimension=0, tiled=True)  147 us
    all_to_all x1, waiting for transfers between devices, shards(): lax.all_to_all(outgoing, 'mp', split_axis=1, concat_axis=1, tiled=True)  40.4 us
    all_to_all x1, waiting for transfers between devices, shards(): lax.all_to_all(outgoing_grad, 'mp', split_axis=1, concat_axis=1, tiled=True)  35.1 us
    dot_general x15, matrix products, contract(): lax.dot_general(left, right, (((left_dim,), (right_dim,)), ((), ())), pre...  24.6 us
    all_to_all x1, starting transfers between devices, shards(): lax.all_to_all(outgoing, 'mp', split_axis=1, concat_axis=1, tiled=True)  12.3 us
    eq x1, other arithmetic, shards(): adjacency = (rowsel[:, None, :] == row_ids).astype(jnp.bfloat16)  9.7 us
    all_to_all x1, starting transfers between devices, shards(): lax.all_to_all(node_features, 'mp', split_axis=1, concat_axis=0, tiled=True)  7.39 us
  transfers between devices with their start and end apart: 5, of which 4 were waited for; matrix products, arithmetic and copies ran while one was open for 14% of the time, Pallas kernels for 0%

commit v1 on v0

--- a/solution.py
+++ b/solution.py
@@ -53,7 +53,12 @@
             global_ids = owner_slots * node_dev + neighbor_row.T
             agg_one_cols = column_mean(node_features, global_ids, live.T, inverse_all)
     own_feats, own_agg_one = (
-        lax.all_to_all(node_features, "mp", split_axis=1, concat_axis=0, tiled=True),
+        jnp.concatenate(
+            lax.all_to_all(
+                jnp.stack(jnp.split(node_features, lax.axis_size("mp"), axis=1)), "mp", 0, 0
+            ),
+            axis=0,
+        ),
         lax.all_to_all(agg_one_cols, "mp", split_axis=1, concat_axis=0, tiled=True),
     )
     pre_one = contract(weights_one[:feat_width], own_feats, 0, 0) + contract(

time: 326 us -> 346 us (1.061)
  local copies, waits for them, and re-layouts: 12.7 us -> 32.5 us
    unnamed x20 -> x35, local copies, waits for them, and re-layouts: 1.25 us -> 21.8 us
  transfers between devices with their start and end apart: 5 -> 5, of which waited for: 4 -> 4; matrix products, arithmetic and copies ran while one was open for 14% -> 13% of each run, Pallas kernels for 0% -> 0%
where the time goes in v1:
time: 346 us; the launch traced here: 345 us
  waiting for transfers between devices  226 us (65%)
  local copies, waits for them, and re-layouts  32.5 us (9%)
  starting transfers between devices  29.5 us (9%)
  matrix products  26 us (8%)
  other arithmetic  15.9 us (5%)
  between operations  14.4 us (4%)
    reduce_scatter x1, waiting for transfers between devices, shards(): lax.psum_scatter(terms, ('dp', 'mp'), scatter_dimension=0, tiled=True)  146 us
    all_to_all x1, waiting for transfers between devices, shards(): lax.all_to_all(outgoing, 'mp', split_axis=1, concat_axis=1, tiled=True)  40.4 us
    all_to_all x1, waiting for transfers between devices, shards(): lax.all_to_all(outgoing_grad, 'mp', split_axis=1, concat_axis=1, tiled=True)  35.1 us
    dot_general x15, matrix products, contract(): lax.dot_general(left, right, (((left_dim,), (right_dim,)), ((), ())), pre...  24.6 us
    unnamed x35, local copies, waits for them, and re-layouts  21.8 us
    all_to_all x1, starting transfers between devices, shards(): lax.all_to_all(outgoing, 'mp', split_axis=1, concat_axis=1, tiled=True)  12.3 us
    eq x1, other arithmetic, shards(): adjacency = (rowsel[:, None, :] == row_ids).astype(jnp.bfloat16)  9.7 us
    all_to_all x1, starting transfers between devices, shards(): lax.all_to_all(jnp.stack(jnp.split(node_features, lax.axis_size('mp'), ax...  7.39 us
  transfers between devices with their start and end apart: 5, of which 4 were waited for; matrix products, arithmetic and copies ran while one was open for 13% of the time, Pallas kernels for 0%

profile of v1, /device:TPU:0, one launch (start us, length us, event | category | flops | bytes accessed | tf_op | source)
XLA Modules:
  0.0 344.5 jit_solution(594095591588740748)
XLA Ops:
  7.2 1.4 constant_dynamic-update-slice_fusion.15
  8.5 1.4 constant_dynamic-update-slice_fusion.14
  9.9 1.4 constant_dynamic-update-slice_fusion.13
  11.3 1.4 constant_dynamic-update-slice_fusion.12
  14.0 1.4 constant_dynamic-update-slice_fusion.10
  16.8 1.4 constant_dynamic-update-slice_fusion.8
  19.5 1.4 constant_dynamic-update-slice_fusion.6
  20.9 1.3 constant_dynamic-update-slice_fusion.5
  22.2 1.4 constant_dynamic-update-slice_fusion.4
  25.0 1.4 constant_dynamic-update-slice_fusion.2
  26.4 1.3 constant_dynamic-update-slice_fusion.1
  27.7 1.4 constant_dynamic-update-slice_fusion
  29.1 7.4 %all-to-all-start = ((bf16[16,32,192]{2,1,0:T(8,128)(2,1)}), bf16[16,32,192]{2,1,0:T(8,128)(2,1)S(1)}, u32[]{:S(2)}, u32[]{:S(2)}) async-start(bf16[16,32,192]{2,1,0:T(8,128)(2,1)} %constant_dynamic-update-slice_fusion), calls=%async_computation | async-start | bytes 524288 | tf_op jit(solution)/shard_map/all_to_all | solution.py:57
  38.0 1.8 select_reduce_fusion
  39.8 9.7 %bitcast_compare_fusion = pred[3072,3072]{1,0:T(32,128)(4,1)} fusion(s32[3072]{0:T(1024)S(1)} %eq.95, s32[16,3072]{1,0:T(8,128)S(1)} %select_reduce_fusion), kind=kLoop, calls=%fused_computation | loop fusion | flops 9437184 | bytes 9646080 | tf_op jit(solution)/shard_map/layer_one_mean/eq | solution.py:47
  49.7 8.5 %fusion.1 = bf16[32,3072]{1,0:T(8,128)(2,1)S(1)} fusion(pred[3072,3072]{1,0:T(32,128)(4,1)} %bitcast_compare_fusion, bf16[32,3072]{1,0:T(8,128)(2,1)S(1)} %copy-done.6, f32[3072]{0:T(1024)S(1)} %convert_divide_fusion), kind=kOutput, calls=%fused_computation.6 | convolution fusion | flops 604176384 | bytes 9842688 | tf_op jit(solution)/shard_map/layer_one_mean/dot_general | solution.py:22
  60.2 6.1 %all-to-all-start.1 = ((bf16[32,16,192]{2,0,1:T(8,128)(2,1)}), bf16[32,16,192]{2,0,1:T(8,128)(2,1)}, u32[]{:S(2)}, u32[]{:S(2)}) async-start(bf16[32,16,192]{2,0,1:T(8,128)(2,1)} %copy.25), calls=%async_computation.1 | async-start | bytes 524288 | tf_op jit(solution)/shard_map/all_to_all | solution.py:62
  67.0 2.2 convolution_convert_fusion
  69.2 2.5 copy.28
  71.7 4.6 %all-to-all-done.1 = bf16[32,16,192]{2,0,1:T(8,128)(2,1)} async-done(((bf16[32,16,192]{2,0,1:T(8,128)(2,1)}), bf16[32,16,192]{2,0,1:T(8,128)(2,1)}, u32[]{:S(2)}, u32[]{:S(2)}) %all-to-all-start.1) | async-done | bytes 196640 | tf_op jit(solution)/shard_map/all_to_all | solution.py:62
  76.3 3.7 %all-to-all-start.3 = ((bf16[512,16,144]{0,2,1:T(8,128)(2,1)}), bf16[512,16,144]{0,2,1:T(8,128)(2,1)S(1)}, u32[]{:S(2)}, u32[]{:S(2)}) async-start(bf16[512,16,144]{0,2,1:T(8,128)(2,1)} %bitcast.31), calls=%async_computation.3 | async-start | bytes 4718592 | tf_op jit(solution)/shard_map/all_to_all | solution.py:105
  82.6 1.3 fusion.21
  83.9 2.4 convolution_convert_fusion.1
  86.3 4.3 %copy.27 = bf16[512,2304]{0,1:T(8,128)(2,1)} copy(bf16[512,2304]{1,0:T(8,128)(2,1)} %convolution_convert_fusion.1) | data formatting | bytes 4718592 | tf_op jit(solution)/shard_map/convert_element_type | solution.py:93
  90.6 35.1 %all-to-all-done.3 = bf16[512,16,144]{0,2,1:T(8,128)(2,1)S(1)} async-done(((bf16[512,16,144]{0,2,1:T(8,128)(2,1)}), bf16[512,16,144]{0,2,1:T(8,128)(2,1)S(1)}, u32[]{:S(2)}, u32[]{:S(2)}) %all-to-all-start.3) | async-done | bytes 2359328 | tf_op jit(solution)/shard_map/all_to_all | solution.py:105
  125.7 12.3 %all-to-all-start.2 = ((bf16[512,16,144]{0,2,1:T(8,128)(2,1)}), bf16[512,16,144]{0,2,1:T(8,128)(2,1)}, u32[]{:S(2)}, u32[]{:S(2)}) async-start(bf16[512,16,144]{0,2,1:T(8,128)(2,1)} %bitcast.27), calls=%async_computation.2 | async-start | bytes 4718592 | tf_op jit(solution)/shard_map/all_to_all | solution.py:94
  138.0 1.3 fusion.42
  139.4 2.0 convolution_bitcast_fusion
  143.3 40.4 %all-to-all-done.2 = bf16[512,16,144]{0,2,1:T(8,128)(2,1)} async-done(((bf16[512,16,144]{0,2,1:T(8,128)(2,1)}), bf16[512,16,144]{0,2,1:T(8,128)(2,1)}, u32[]{:S(2)}, u32[]{:S(2)}) %all-to-all-start.2) | async-done | bytes 2359328 | tf_op jit(solution)/shard_map/all_to_all | solution.py:94
  183.7 2.6 fusion.26
  186.7 2.4 pad_maximum_fusion
  191.5 146.1 %reduce-scatter.2.cloned.1.call-done = f32[64,512]{1,0:T(8,128)} async-done(((f32[2048,512]{1,0:T(8,128)}), f32[64,512]{1,0:T(8,128)}) %reduce-scatter.2.cloned.1.call-update) | async-done | bytes 131088 | tf_op jit(solution)/shard_map/reduce_scatter | solution.py:118
  (55 shorter events, 16.6 us)
Async XLA Ops:
  7.2 59.8 %copy-start = (bf16[192,512]{1,0:T(8,128)(2,1)S(1)}, bf16[192,512]{1,0:T(8,128)(2,1)}, u32[]{:S(2)}) copy-start(bf16[192,512]{1,0:T(8,128)(2,1)} %param.13) | copy-start | bytes 589828
  29.1 31.1 %all-to-all-start = ((bf16[16,32,192]{2,1,0:T(8,128)(2,1)}), bf16[16,32,192]{2,1,0:T(8,128)(2,1)S(1)}, u32[]{:S(2)}, u32[]{:S(2)}) async-start(bf16[16,32,192]{2,1,0:T(8,128)(2,1)} %constant_dynamic-update-slice_fusion), calls=%async_computation | async-start | bytes 524288 | tf_op jit(solution)/shard_map/all_to_all | solution.py:57
  39.8 9.9 %copy-start.6 = (bf16[32,3072]{1,0:T(8,128)(2,1)S(1)}, bf16[32,3072]{1,0:T(8,128)(2,1)}, u32[]{:S(2)}) copy-start(bf16[32,3072]{1,0:T(8,128)(2,1)} %param.7) | copy-start | bytes 589828
  58.8 7.7 %copy-start.1 = (s32[16,16,192]{2,1,0:T(8,128)}, s32[16,16,192]{2,1,0:T(8,128)S(1)}, u32[]{:S(2)}) copy-start(s32[16,16,192]{2,1,0:T(8,128)S(1)} %reduce_max.12) | copy-start | bytes 589828
  60.1 6.4 %copy-start.7 = (s32[256,192]{1,0:T(8,128)}, s32[256,192]{1,0:T(8,128)S(1)}, u32[]{:S(2)}) copy-start(s32[256,192]{1,0:T(8,128)S(1)} %copy.26) | copy-start | bytes 589828
  60.2 16.2 %all-to-all-start.1 = ((bf16[32,16,192]{2,0,1:T(8,128)(2,1)}), bf16[32,16,192]{2,0,1:T(8,128)(2,1)}, u32[]{:S(2)}, u32[]{:S(2)}) async-start(bf16[32,16,192]{2,0,1:T(8,128)(2,1)} %copy.25), calls=%async_computation.1 | async-start | bytes 524288 | tf_op jit(solution)/shard_map/all_to_all | solution.py:62
  76.3 49.3 %all-to-all-start.3 = ((bf16[512,16,144]{0,2,1:T(8,128)(2,1)}), bf16[512,16,144]{0,2,1:T(8,128)(2,1)S(1)}, u32[]{:S(2)}, u32[]{:S(2)}) async-start(bf16[512,16,144]{0,2,1:T(8,128)(2,1)} %bitcast.31), calls=%async_computation.3 | async-start | bytes 4718592 | tf_op jit(solution)/shard_map/all_to_all | solution.py:105
  80.1 2.2 copy-start.2
  82.3 1.7 copy-start.8
  125.7 58.0 %all-to-all-start.2 = ((bf16[512,16,144]{0,2,1:T(8,128)(2,1)}), bf16[512,16,144]{0,2,1:T(8,128)(2,1)}, u32[]{:S(2)}, u32[]{:S(2)}) async-start(bf16[512,16,144]{0,2,1:T(8,128)(2,1)} %bitcast.27), calls=%async_computation.2 | async-start | bytes 4718592 | tf_op jit(solution)/shard_map/all_to_all | solution.py:94
  138.0 199.7 %reduce-scatter.2.cloned.1.call-start = ((), (), s32[]{:S(2)}) async-start(), calls=%async_computation.5 | async-start | bytes 4325376 | tf_op jit(solution)/shard_map/reduce_scatter | solution.py:118
  139.4 2.0 copy-start.3
  183.7 3.0 copy-start.5
  189.1 1.2 copy-start.4
Sparse Core Ops, SparseCore 0:
  189.2 148.4 reduce-scatter.1
